TPU v7x, 512 devices: a whole 4x4x16 slice. The times are simulated.
512 devices in a mesh: exp: 16 (over z), sky: 32 (over y, x, core).
Axes of the slice: x: 4, y: 4, z: 16, core: 2. Of those that a mesh axis runs over, the one named last changes fastest.
Arguments:
- sky_start: float32 [16, 128, 4096], P(None, None, 'sky'), may hold values from -6 to 6
- exposures: bfloat16 [16, 1024, 2, 128, 128], P('exp', 'sky'), may hold values from -16 to 16
- weights: bfloat16 [16, 1024, 2], P('exp', 'sky'), may hold values from 0.5 to 2
- footprint_owner: int32 [16, 1024, 1], P('exp', 'sky'), may hold values from 0 to 31; in each aligned block of 32 rows (0 to 31, 32 to 63, ..., all dimensions but the last counted through in order) at most 2 rows name the same one
- footprint_row: int32 [16, 1024], P('exp', 'sky'), may hold values from 0 to 15
- kernel_index: int32 [16, 1024, 2, 2], P('exp', 'sky'), may hold values from 0 to 7
- kernels: bfloat16 [8, 128, 128], replicated, may hold values from -1 to 1
Outputs:
- sky_image: float32 [16, 128, 4096], P(None, None, 'sky')
Inputs may be any that keep to these rules, and one draw needn't show every extreme that they name: `footprint_owner`: the 32 footprint tiles of one device name one tile column at most 2 times, and some tile column exactly 2 times.
All inputs are finite; a program needn't handle non-finite values.
Results may differ from a plain program's by a relative error of at most 0.0035.
Values may be sent and summed in bfloat16 or wider, within the bound.
No kernel may reach another device: no remote copies, remote signals or barrier semaphores. Data moves between devices by JAX's collectives and lax.ppermute only.
A program may use at most 128 MiB of HBM per device.

v0:
```python
import jax
import jax.numpy as jnp
from jax import lax
from jax.sharding import PartitionSpec as P

ITERS = 2
weight_ceiling = 2.0


def padded_2(cells, sides, width):
    for axis, dim in sides:
        count = lax.axis_size(axis)
        ends = count - 1
        head = lax.slice_in_dim(cells, 0, width, axis=dim)
        tail = lax.slice_in_dim(cells, cells.shape[dim] - width, cells.shape[dim], axis=dim)
        cells = jnp.concatenate(
            [
                lax.ppermute(tail, axis, [(i, (i + 1) % count) for i in range(ends)]),
                cells,
                lax.ppermute(head, axis, [((i + 1) % count, i) for i in range(ends)]),
            ],
            axis=dim,
        )
    return cells


def pick_kernels(kernel_ids, kernels):
    table_size = kernels.shape[0]
    tile_edge = kernels.shape[1]
    onehot = (kernel_ids[..., None] == jnp.arange(table_size, dtype=jnp.int32)).astype(jnp.bfloat16)
    onehot = onehot.reshape(-1, table_size)
    selected = jnp.dot(onehot, kernels.reshape(table_size, -1), preferred_element_type=jnp.float32)
    selected = selected.astype(jnp.bfloat16).reshape(kernel_ids.shape + (tile_edge, tile_edge))
    return (selected[..., 0, :, :], selected[..., 1, :, :])


def adjoint_tiles(fetched, left_kernels, right_kernels, tile_weights, observed):
    left_product = jnp.einsum(
        "fetu,fuv->fetv", left_kernels, fetched, preferred_element_type=jnp.float32
    ).astype(jnp.bfloat16)
    predicted = jnp.einsum(
        "fetv,fewv->fetw", left_product, right_kernels, preferred_element_type=jnp.float32
    )
    residual = tile_weights.astype(jnp.float32)[..., None, None] * (
        predicted - observed.astype(jnp.float32)
    )
    residual = residual.astype(jnp.bfloat16)
    back_product = jnp.einsum(
        "feut,feuw->fetw", left_kernels, residual, preferred_element_type=jnp.float32
    ).astype(jnp.bfloat16)
    summed = jnp.sum(
        jnp.einsum(
            "fetw,fewv->fetv", back_product, right_kernels, preferred_element_type=jnp.float32
        ),
        axis=1,
    )
    return summed.astype(jnp.bfloat16)


def laplace_image(padded):
    image_rows = padded.reshape(padded.shape[0] * padded.shape[1], padded.shape[2])
    center = image_rows[:, 1:-1]
    vertical = jnp.pad(center, ((1, 1), (0, 0)))
    laplacian = 4.0 * center - image_rows[:, :-2] - image_rows[:, 2:] - vertical[:-2] - vertical[2:]
    return laplacian.reshape(padded.shape[0], padded.shape[1], padded.shape[2] - 2)


def per_device(
    sky_start, exposures, weights, footprint_owner, footprint_row, kernel_index, kernels
):
    sky_rows = sky_start.shape[0]
    tile_edge = sky_start.shape[1]
    foot_tiles = footprint_row.shape[1]
    expo_count = exposures.shape[2]
    n_sky = lax.axis_size("sky")
    n_exp = lax.axis_size("exp")
    capacity = max(2, 3 * foot_tiles // (2 * n_sky))
    slot_count = n_sky * capacity
    prior_weight = n_exp * foot_tiles * expo_count / (8.0 * sky_rows)
    owner_ids = footprint_owner[0, :, 0]
    tile_rows = footprint_row[0]
    onehot_owner = (owner_ids[:, None] == jnp.arange(n_sky, dtype=jnp.int32)[None, :]).astype(
        jnp.int32
    )
    ranks = jnp.sum((jnp.cumsum(onehot_owner, axis=0) - onehot_owner) * onehot_owner, axis=1)
    slot_of = owner_ids * capacity + ranks
    packing = jnp.arange(slot_count, dtype=jnp.int32)[:, None] == slot_of[None, :]
    requested = jnp.sum(jnp.where(packing, tile_rows[None, :] + 1, 0), axis=1) - 1
    slot_source = jnp.sum(jnp.where(packing, jnp.arange(foot_tiles)[None, :] + 1, 0), axis=1) - 1
    slot_source = jnp.where(slot_source < 0, foot_tiles, slot_source)
    observed = exposures[0]
    tile_weights = weights[0]
    kernel_ids = kernel_index[0]
    incoming = lax.all_to_all(requested, "sky", split_axis=0, concat_axis=0, tiled=True)
    left_kernels, right_kernels = pick_kernels(kernel_ids, kernels)
    receive_map = jnp.arange(sky_rows, dtype=jnp.int32)[:, None] == incoming[None, :]
    local_counts = float(expo_count) * jnp.sum(receive_map.astype(jnp.float32), axis=1)
    receive_half = receive_map.astype(jnp.bfloat16)
    safe_rows = jnp.maximum(incoming, 0)
    rows_per = sky_rows // n_exp
    own_rows = lax.axis_index("exp") * rows_per
    count_block = jnp.broadcast_to(
        local_counts.astype(jnp.bfloat16)[None, :, None], (n_exp, sky_rows, tile_edge)
    )
    half_edge = tile_edge // 2

    def exchange(outgoing_rows, extra, arrived_already=False):
        arrived = outgoing_rows
        if not arrived_already:
            arrived = lax.all_to_all(outgoing_rows, "sky", split_axis=0, concat_axis=0, tiled=True)
        partial_value = jnp.einsum(
            "rj,juv->ruv", receive_half, arrived, preferred_element_type=jnp.float32
        )
        payload = partial_value.astype(jnp.bfloat16).reshape(
            n_exp, rows_per * outgoing_rows.shape[1], tile_edge
        )
        if extra is not None:
            payload = jnp.concatenate([payload, extra], axis=1)
        row_parts = lax.all_to_all(payload, "exp", split_axis=0, concat_axis=0, tiled=True)
        return jnp.sum(row_parts.astype(jnp.float32).reshape((n_exp,) + payload.shape[1:]), axis=0)

    def fetch(part):
        replies = lax.all_to_all(
            part.astype(jnp.bfloat16)[safe_rows], "sky", split_axis=0, concat_axis=0, tiled=True
        )
        return replies[slot_of]

    def gather_scaled(summed, own_denominator):
        piece_edge = summed.shape[0] // rows_per
        own_total = summed.reshape(rows_per, piece_edge, tile_edge)
        scaled = (own_total / own_denominator[:, None, None]).astype(jnp.bfloat16)
        return scaled

    sky_now = sky_start
    fetched = None
    for iteration in range(ITERS):
        if fetched is None:
            fetched = fetch(sky_now)
        adjoint = adjoint_tiles(fetched, left_kernels, right_kernels, tile_weights, observed)
        padded_adjoint = jnp.concatenate(
            [adjoint, jnp.zeros((1, tile_edge, tile_edge), adjoint.dtype)], axis=0
        )
        outgoing = padded_adjoint[slot_source]
        laplacian = laplace_image(padded_2(sky_now, (("sky", 2),), 1))
        if iteration == 0:
            summed = exchange(outgoing[:, :half_edge], count_block)
            counts = summed[rows_per * half_edge :, 0]
            denominator = weight_ceiling * counts + 8.0 * prior_weight
            own_denominator = lax.dynamic_slice_in_dim(denominator, own_rows, rows_per)
            summed_head = summed[: rows_per * half_edge]
            smooth = prior_weight * laplacian / denominator[:, None, None]
        else:
            smooth = prior_weight * laplacian / denominator[:, None, None]
            if iteration + 1 == ITERS:
                scaled = gather_scaled(exchange(outgoing, None), own_denominator)
                gathered = lax.all_gather(scaled, "exp", axis=0, tiled=True)
                sky_now = sky_now - (gathered.astype(jnp.float32) + smooth)
                continue
            summed_head = exchange(outgoing[:, :half_edge], None)
        scaled_head = gather_scaled(summed_head, own_denominator)
        scaled_head, outgoing_tail = lax.optimization_barrier(
            (scaled_head, outgoing[:, half_edge:])
        )
        gathered_head = lax.all_gather(scaled_head, "exp", axis=0, tiled=True)
        arrived_tail = lax.all_to_all(outgoing_tail, "sky", split_axis=0, concat_axis=0, tiled=True)
        gathered_head, arrived_tail = lax.optimization_barrier((gathered_head, arrived_tail))
        scaled_tail = gather_scaled(exchange(arrived_tail, None, True), own_denominator)
        sky_head = sky_now[:, :half_edge] - (
            gathered_head.astype(jnp.float32) + smooth[:, :half_edge]
        )
        if iteration + 1 == ITERS:
            gathered_tail = lax.all_gather(scaled_tail, "exp", axis=0, tiled=True)
            sky_tail = sky_now[:, half_edge:] - (
                gathered_tail.astype(jnp.float32) + smooth[:, half_edge:]
            )
            sky_now = jnp.concatenate([sky_head, sky_tail], axis=1)
            continue
        request_head = sky_head.astype(jnp.bfloat16)[safe_rows]
        request_head, scaled_tail = lax.optimization_barrier((request_head, scaled_tail))
        gathered_tail = lax.all_gather(scaled_tail, "exp", axis=0, tiled=True)
        fetched_head = lax.all_to_all(request_head, "sky", split_axis=0, concat_axis=0, tiled=True)[
            slot_of
        ]
        gathered_tail, fetched_head = lax.optimization_barrier((gathered_tail, fetched_head))
        sky_tail = sky_now[:, half_edge:] - (
            gathered_tail.astype(jnp.float32) + smooth[:, half_edge:]
        )
        fetched = jnp.concatenate([fetched_head, fetch(sky_tail)], axis=1)
        sky_now = jnp.concatenate([sky_head, sky_tail], axis=1)
    return sky_now


def solution(mesh):
    in_specs = (
        P(None, None, "sky"),
        P("exp", "sky", None, None, None),
        P("exp", "sky", None),
        P("exp", "sky", None),
        P("exp", "sky"),
        P("exp", "sky", None, None),
        P(),
    )
    out_specs = P(None, None, "sky")
    return jax.shard_map(
        per_device, mesh=mesh, in_specs=in_specs, out_specs=out_specs, check_vma=False
    )
```

profile of v0, /device:TPU:2, one launch (start us, length us, event | category | flops | bytes accessed | tf_op | source)
XLA Modules:
  0.0 392.2 jit_solution(12822003709473119195)
XLA Ops:
  3.8 9.4 %all-to-all-start = ((s32[32,2,1]{1,2,0:T(1,128)}), s32[32,2,1]{1,2,0:T(1,128)S(1)}, u32[]{:S(2)}, u32[]{:S(2)}) async-start(s32[32,2,1]{1,2,0:T(1,128)} %bitcast.2), calls=%async_computation | async-start | bytes 32768 | tf_op jit(solution)/shard_map/all_to_all | solution.py:94
  14.5 4.9 %all-to-all-done = s32[32,2,1]{1,2,0:T(1,128)S(1)} async-done(((s32[32,2,1]{1,2,0:T(1,128)}), s32[32,2,1]{1,2,0:T(1,128)S(1)}, u32[]{:S(2)}, u32[]{:S(2)}) %all-to-all-start) | async-done | bytes 288 | tf_op jit(solution)/shard_map/all_to_all | solution.py:94
  20.7 2.1 gather_fusion
  22.9 5.2 %all-to-all-start.1 = ((bf16[64,128,128]{2,1,0:T(8,128)(2,1)}), bf16[64,128,128]{2,1,0:T(8,128)(2,1)S(1)}, u32[]{:S(2)}, u32[]{:S(2)}) async-start(bf16[64,128,128]{2,1,0:T(8,128)(2,1)} %gather_fusion), calls=%async_computation.1 | async-start | bytes 4194304 | tf_op jit(solution)/shard_map/all_to_all | solution.py:123
  29.8 3.2 copy.72
  33.0 23.1 %all-to-all-done.1 = bf16[64,128,128]{2,1,0:T(8,128)(2,1)S(1)} async-done(((bf16[64,128,128]{2,1,0:T(8,128)(2,1)}), bf16[64,128,128]{2,1,0:T(8,128)(2,1)S(1)}, u32[]{:S(2)}, u32[]{:S(2)}) %all-to-all-start.1) | async-done | bytes 2097184 | tf_op jit(solution)/shard_map/all_to_all | solution.py:123
  56.8 6.3 %fusion.1 = bf16[32,2,128,128]{3,2,1,0:T(8,128)(2,1)} fusion(bf16[1,32,2,128,128]{4,3,2,1,0:T(8,128)(2,1)} %param.8, f32[32,2]{1,0:T(8,128)S(1)} %copy.43, bf16[32,2,2,128,128]{4,3,2,1,0:T(8,128)(2,1)} %bitcast.93, bf16[32,128,128]{2,1,0:T(8,128)(2,1)S(1)} %gather_fusion.1), kind=kOutput, calls=%fused_computation.12 | convolution fusion | flops 542113792 | bytes 9437440 | tf_op jit(solution)/shard_map/fetv,fewv->fetw/dot_general | solution.py:41
  63.2 4.3 %bitcast_convert_fusion.1 = bf16[32,128,128]{2,1,0:T(8,128)(2,1)S(1)} fusion(bf16[32,2,128,128]{3,2,1,0:T(8,128)(2,1)} %fusion.1, bf16[32,2,2,128,128]{4,3,2,1,0:T(8,128)(2,1)} %bitcast.94), kind=kOutput, calls=%fused_computation.21 | convolution fusion | flops 538443776 | bytes 7340032 | tf_op jit(solution)/shard_map/fetw,fewv->fetv/dot_general | solution.py:52
  70.0 5.9 %all-to-all-start.2 = ((bf16[64,64,128]{2,1,0:T(8,128)(2,1)}), bf16[64,64,128]{2,1,0:T(8,128)(2,1)S(1)}, u32[]{:S(2)}, u32[]{:S(2)}) async-start(bf16[64,64,128]{2,1,0:T(8,128)(2,1)} %get-tuple-element.30), calls=%async_computation.2 | async-start | bytes 2097152 | tf_op jit(solution)/shard_map/all_to_all | solution.py:110
  76.3 15.9 %all-to-all-done.2 = bf16[64,64,128]{2,1,0:T(8,128)(2,1)S(1)} async-done(((bf16[64,64,128]{2,1,0:T(8,128)(2,1)}), bf16[64,64,128]{2,1,0:T(8,128)(2,1)S(1)}, u32[]{:S(2)}, u32[]{:S(2)}) %all-to-all-start.2) | async-done | bytes 1048608 | tf_op jit(solution)/shard_map/all_to_all | solution.py:110
  93.9 13.3 %all-to-all-start.3 = ((bf16[16,80,128]{2,1,0:T(8,128)(2,1)}), bf16[16,80,128]{2,1,0:T(8,128)(2,1)S(1)}, u32[]{:S(2)}, u32[]{:S(2)}) async-start(bf16[16,80,128]{2,1,0:T(8,128)(2,1)} %copy.47), calls=%async_computation.3 | async-start | bytes 655360 | tf_op jit(solution)/shard_map/all_to_all | solution.py:119
  107.2 21.4 %all-to-all-done.3 = bf16[16,80,128]{2,1,0:T(8,128)(2,1)S(1)} async-done(((bf16[16,80,128]{2,1,0:T(8,128)(2,1)}), bf16[16,80,128]{2,1,0:T(8,128)(2,1)S(1)}, u32[]{:S(2)}, u32[]{:S(2)}) %all-to-all-start.3) | async-done | bytes 327712 | tf_op jit(solution)/shard_map/all_to_all | solution.py:119
  129.9 5.6 %all-to-all-start.4 = ((bf16[64,64,128]{2,1,0:T(8,128)(2,1)}), bf16[64,64,128]{2,1,0:T(8,128)(2,1)}, u32[]{:S(2)}, u32[]{:S(2)}) async-start(bf16[64,64,128]{2,1,0:T(8,128)(2,1)} %get-tuple-element.14), calls=%async_computation.4 | async-start | bytes 2097152 | tf_op jit(solution)/shard_map/all_to_all | solution.py:165
  138.6 2.5 collective-permute-start
  141.1 6.4 %collective-permute-done.1 = f32[16,128,1]{1,0,2:T(8,128)S(1)} collective-permute-done((f32[16,128,1]{1,0,2:T(8,128)S(1)}, f32[16,128,1]{1,0,2:T(8,128)S(1)}, u32[]{:S(2)}, u32[]{:S(2)}) %collective-permute-start.1) | collective-permute-done | bytes 8224 | tf_op jit(solution)/shard_map/ppermute | solution.py:20
  150.2 2.4 pad_maximum_fusion
  153.9 33.8 %all_gather.9 = bf16[16,64,128]{2,1,0:T(8,128)(2,1)} all-gather(bf16[1,64,128]{2,1,0:T(8,128)(2,1)S(1)} %fusion.53), channel_id=1, replica_groups=mesh['exp'=16,'sky'=32] {'exp'}, dimensions={0}, use_global_device_ids=true | all-gather | bytes 278528 | tf_op jit(solution)/shard_map/all_gather | solution.py:164
  190.5 4.5 %all-to-all-start.5 = ((bf16[16,64,128]{2,1,0:T(8,128)(2,1)}), bf16[16,64,128]{2,1,0:T(8,128)(2,1)S(1)}, u32[]{:S(2)}, u32[]{:S(2)}) async-start(bf16[16,64,128]{2,1,0:T(8,128)(2,1)} %copy.53), calls=%async_computation.5 | async-start | bytes 524288 | tf_op jit(solution)/shard_map/all_to_all | solution.py:119
  194.9 2.5 fusion.36
  201.0 8.2 %all-to-all-done.5 = bf16[16,64,128]{2,1,0:T(8,128)(2,1)S(1)} async-done(((bf16[16,64,128]{2,1,0:T(8,128)(2,1)}), bf16[16,64,128]{2,1,0:T(8,128)(2,1)S(1)}, u32[]{:S(2)}, u32[]{:S(2)}) %all-to-all-start.5) | async-done | bytes 262176 | tf_op jit(solution)/shard_map/all_to_all | solution.py:119
  209.8 7.9 %all-to-all-start.6 = ((bf16[64,64,128]{2,1,0:T(8,128)(2,1)}), bf16[64,64,128]{2,1,0:T(8,128)(2,1)S(1)}, u32[]{:S(2)}, u32[]{:S(2)}) async-start(bf16[64,64,128]{2,1,0:T(8,128)(2,1)} %gather_fusion.3), calls=%async_computation.6 | async-start | bytes 2097152 | tf_op jit(solution)/shard_map/all_to_all | solution.py:181
  217.7 31.1 %all_gather.10 = bf16[16,64,128]{2,1,0:T(8,128)(2,1)S(1)} all-gather(bf16[1,64,128]{2,1,0:T(8,128)(2,1)S(1)} %fusion.52), channel_id=1, replica_groups=mesh['exp'=16,'sky'=32] {'exp'}, dimensions={0}, use_global_device_ids=true | all-gather | bytes 278528 | tf_op jit(solution)/shard_map/all_gather | solution.py:180
  251.9 23.4 %all_to_all.51 = bf16[64,64,128]{2,1,0:T(8,128)(2,1)S(1)} all-to-all(bf16[64,64,128]{2,1,0:T(8,128)(2,1)S(1)} %gather_fusion.5), channel_id=1, replica_groups=mesh['exp'=16,'sky'=32] {'sky'}, dimensions={0} | all-to-all | bytes 2097152 | tf_op jit(solution)/shard_map/all_to_all | solution.py:123
  276.0 6.3 %fusion.3 = bf16[32,2,128,128]{3,2,1,0:T(8,128)(2,1)} fusion(bf16[1,32,2,128,128]{4,3,2,1,0:T(8,128)(2,1)} %param.8, f32[32,2]{1,0:T(8,128)S(1)} %copy.43, bf16[32,2,2,128,128]{4,3,2,1,0:T(8,128)(2,1)} %bitcast.95, bf16[32,64,128]{2,1,0:T(8,128)(2,1)S(1)} %gather_fusion.6, bf16[32,64,128]{2,1,0:T(8,128)(2,1)S(1)} %copy-done.4), kind=kOutput, calls=%fused_computation.14 | convolution fusion | flops 544210944 | bytes 9437440 | tf_op jit(solution)/shard_map/fetv,fewv->fetw/dot_general | solution.py:41
  282.3 4.3 %bitcast_convert_fusion = bf16[32,128,128]{2,1,0:T(8,128)(2,1)S(1)} fusion(bf16[32,2,128,128]{3,2,1,0:T(8,128)(2,1)} %fusion.3, bf16[32,2,2,128,128]{4,3,2,1,0:T(8,128)(2,1)} %bitcast.96), kind=kOutput, calls=%fused_computation.20 | convolution fusion | flops 538443776 | bytes 7340032 | tf_op jit(solution)/shard_map/fetw,fewv->fetv/dot_general | solution.py:52
  287.7 31.9 %all_to_all.52 = bf16[64,128,128]{2,1,0:T(8,128)(2,1)S(1)} all-to-all(bf16[64,128,128]{2,1,0:T(8,128)(2,1)S(1)} %gather_fusion.7), channel_id=1, replica_groups=mesh['exp'=16,'sky'=32] {'sky'}, dimensions={0} | all-to-all | bytes 4194304 | tf_op jit(solution)/shard_map/all_to_all | solution.py:110
  321.8 4.3 %all-to-all-start.9 = ((bf16[16,128,128]{2,1,0:T(8,128)(2,1)}), bf16[16,128,128]{2,1,0:T(8,128)(2,1)}, u32[]{:S(2)}, u32[]{:S(2)}) async-start(bf16[16,128,128]{2,1,0:T(8,128)(2,1)} %copy.56), calls=%async_computation.9 | async-start | bytes 1048576 | tf_op jit(solution)/shard_map/all_to_all | solution.py:119
  326.8 3.1 collective-permute-start.3
  330.2 2.1 collective-permute-start.2
  332.7 2.4 collective-permute-done.2
  337.2 18.3 %all-to-all-done.9 = bf16[16,128,128]{2,1,0:T(8,128)(2,1)} async-done(((bf16[16,128,128]{2,1,0:T(8,128)(2,1)}), bf16[16,128,128]{2,1,0:T(8,128)(2,1)}, u32[]{:S(2)}, u32[]{:S(2)}) %all-to-all-start.9) | async-done | bytes 524320 | tf_op jit(solution)/shard_map/all_to_all | solution.py:119
  357.2 33.7 %all-gather = bf16[2048,128]{1,0:T(8,128)(2,1)S(1)} all-gather(bf16[128,128]{1,0:T(8,128)(2,1)S(1)} %divide_convert_fusion), channel_id=2, replica_groups=mesh['exp'=16,'sky'=32] {'exp'}, dimensions={0}, use_global_device_ids=true | all-gather | bytes 557056 | tf_op jit(solution)/shard_map/all_gather | solution.py:156
  (92 shorter events, 42.0 us)
Async XLA Ops:
  3.8 15.6 %all-to-all-start = ((s32[32,2,1]{1,2,0:T(1,128)}), s32[32,2,1]{1,2,0:T(1,128)S(1)}, u32[]{:S(2)}, u32[]{:S(2)}) async-start(s32[32,2,1]{1,2,0:T(1,128)} %bitcast.2), calls=%async_computation | async-start | bytes 32768 | tf_op jit(solution)/shard_map/all_to_all | solution.py:94
  22.8 5.3 %copy-start.8 = (bf16[1,32,2]{1,2,0:T(2,128)(2,1)S(1)}, bf16[1,32,2]{1,2,0:T(2,128)(2,1)}, u32[]{:S(2)}) copy-start(bf16[1,32,2]{1,2,0:T(2,128)(2,1)} %param.9) | copy-start | bytes 388
  22.8 5.4 %copy-start.7 = (s32[1,32,2,2]{1,3,2,0:T(2,128)S(1)}, s32[1,32,2,2]{1,3,2,0:T(2,128)}, u32[]{:S(2)}) copy-start(s32[1,32,2,2]{1,3,2,0:T(2,128)} %param.12) | copy-start | bytes 1540
  22.8 5.6 %copy-start.5 = (bf16[8,128,128]{2,1,0:T(8,128)(2,1)S(1)}, bf16[8,128,128]{2,1,0:T(8,128)(2,1)}, u32[]{:S(2)}) copy-start(bf16[8,128,128]{2,1,0:T(8,128)(2,1)} %param.13) | copy-start | bytes 786436
  22.9 33.2 %all-to-all-start.1 = ((bf16[64,128,128]{2,1,0:T(8,128)(2,1)}), bf16[64,128,128]{2,1,0:T(8,128)(2,1)S(1)}, u32[]{:S(2)}, u32[]{:S(2)}) async-start(bf16[64,128,128]{2,1,0:T(8,128)(2,1)} %gather_fusion), calls=%async_computation.1 | async-start | bytes 4194304 | tf_op jit(solution)/shard_map/all_to_all | solution.py:123
  29.8 3.2 copy-start.6
  70.0 22.2 %all-to-all-start.2 = ((bf16[64,64,128]{2,1,0:T(8,128)(2,1)}), bf16[64,64,128]{2,1,0:T(8,128)(2,1)S(1)}, u32[]{:S(2)}, u32[]{:S(2)}) async-start(bf16[64,64,128]{2,1,0:T(8,128)(2,1)} %get-tuple-element.30), calls=%async_computation.2 | async-start | bytes 2097152 | tf_op jit(solution)/shard_map/all_to_all | solution.py:110
  92.9 42.7 %copy-start = (f32[16,128,128]{2,1,0:T(8,128)S(1)}, f32[16,128,128]{2,1,0:T(8,128)}, u32[]{:S(2)}) copy-start(f32[16,128,128]{2,1,0:T(8,128)} %param.7) | copy-start | bytes 3145732
  93.9 34.7 %all-to-all-start.3 = ((bf16[16,80,128]{2,1,0:T(8,128)(2,1)}), bf16[16,80,128]{2,1,0:T(8,128)(2,1)S(1)}, u32[]{:S(2)}, u32[]{:S(2)}) async-start(bf16[16,80,128]{2,1,0:T(8,128)(2,1)} %copy.47), calls=%async_computation.3 | async-start | bytes 655360 | tf_op jit(solution)/shard_map/all_to_all | solution.py:119
  129.9 57.8 %all-to-all-start.4 = ((bf16[64,64,128]{2,1,0:T(8,128)(2,1)}), bf16[64,64,128]{2,1,0:T(8,128)(2,1)}, u32[]{:S(2)}, u32[]{:S(2)}) async-start(bf16[64,64,128]{2,1,0:T(8,128)(2,1)} %get-tuple-element.14), calls=%async_computation.4 | async-start | bytes 2097152 | tf_op jit(solution)/shard_map/all_to_all | solution.py:165
  136.3 11.2 %collective-permute-start.1 = (f32[16,128,1]{1,0,2:T(8,128)S(1)}, f32[16,128,1]{1,0,2:T(8,128)S(1)}, u32[]{:S(2)}, u32[]{:S(2)}) collective-permute-start(f32[16,128,1]{1,0,2:T(8,128)S(1)} %copy.70), channel_id=1, source_target_pairs={{1,0},{2,1},{3,2},{4,3},{5,4},{6,5},{7,6},{8,7},{9,8},{10,9},{11,1... | collective-permute-start | bytes 24584 | tf_op jit(solution)/shard_map/ppermute | solution.py:20
  138.6 10.2 %collective-permute-start = (f32[16,128,1]{1,0,2:T(8,128)S(1)}, f32[16,128,1]{1,0,2:T(8,128)S(1)}, u32[]{:S(2)}, u32[]{:S(2)}) collective-permute-start(f32[16,128,1]{1,0,2:T(8,128)S(1)} %copy.69), channel_id=1, source_target_pairs={{0,1},{1,2},{2,3},{3,4},{4,5},{5,6},{6,7},{7,8},{8,9},{9,10},{10,1... | collective-permute-start | bytes 24584 | tf_op jit(solution)/shard_map/ppermute | solution.py:18
  190.5 18.7 %all-to-all-start.5 = ((bf16[16,64,128]{2,1,0:T(8,128)(2,1)}), bf16[16,64,128]{2,1,0:T(8,128)(2,1)S(1)}, u32[]{:S(2)}, u32[]{:S(2)}) async-start(bf16[16,64,128]{2,1,0:T(8,128)(2,1)} %copy.53), calls=%async_computation.5 | async-start | bytes 524288 | tf_op jit(solution)/shard_map/all_to_all | solution.py:119
  197.5 1.0 copy-start.3
  209.8 39.0 %all-to-all-start.6 = ((bf16[64,64,128]{2,1,0:T(8,128)(2,1)}), bf16[64,64,128]{2,1,0:T(8,128)(2,1)S(1)}, u32[]{:S(2)}, u32[]{:S(2)}) async-start(bf16[64,64,128]{2,1,0:T(8,128)(2,1)} %gather_fusion.3), calls=%async_computation.6 | async-start | bytes 2097152 | tf_op jit(solution)/shard_map/all_to_all | solution.py:181
  251.9 24.1 %copy-start.4 = (bf16[32,64,128]{2,1,0:T(8,128)(2,1)S(1)}, bf16[32,64,128]{2,1,0:T(8,128)(2,1)}, u32[]{:S(2)}) copy-start(bf16[32,64,128]{2,1,0:T(8,128)(2,1)} %gather_fusion.4) | copy-start | bytes 1572868
  319.6 6.5 %copy-start.1 = (f32[16,64,128]{2,1,0:T(8,128)S(1)}, f32[16,64,128]{2,1,0:T(8,128)}, u32[]{:S(2)}) copy-start(f32[16,64,128]{2,1,0:T(8,128)} %get-tuple-element.28) | copy-start | bytes 1572868
  319.6 6.5 %copy-start.2 = (f32[16,64,128]{2,1,0:T(8,128)S(1)}, f32[16,64,128]{2,1,0:T(8,128)}, u32[]{:S(2)}) copy-start(f32[16,64,128]{2,1,0:T(8,128)} %get-tuple-element.26) | copy-start | bytes 1572868
  321.8 33.7 %all-to-all-start.9 = ((bf16[16,128,128]{2,1,0:T(8,128)(2,1)}), bf16[16,128,128]{2,1,0:T(8,128)(2,1)}, u32[]{:S(2)}, u32[]{:S(2)}) async-start(bf16[16,128,128]{2,1,0:T(8,128)(2,1)} %copy.56), calls=%async_computation.9 | async-start | bytes 1048576 | tf_op jit(solution)/shard_map/all_to_all | solution.py:119
  326.8 5.5 %collective-permute-start.3 = (f32[16,128,1]{1,0,2:T(8,128)S(1)}, f32[16,128,1]{1,0,2:T(8,128)S(1)}, u32[]{:S(2)}, u32[]{:S(2)}) collective-permute-start(f32[16,128,1]{1,0,2:T(8,128)S(1)} %copy.58), channel_id=1, source_target_pairs={{1,0},{2,1},{3,2},{4,3},{5,4},{6,5},{7,6},{8,7},{9,8},{10,9},{11,1... | collective-permute-start | bytes 24584 | tf_op jit(solution)/shard_map/ppermute | solution.py:20
  330.2 5.0 %collective-permute-start.2 = (f32[16,128,1]{1,0,2:T(8,128)S(1)}, f32[16,128,1]{1,0,2:T(8,128)S(1)}, u32[]{:S(2)}, u32[]{:S(2)}) collective-permute-start(f32[16,128,1]{1,0,2:T(8,128)S(1)} %copy.57), channel_id=1, source_target_pairs={{0,1},{1,2},{2,3},{3,4},{4,5},{5,6},{6,7},{7,8},{8,9},{9,10},{10,1... | collective-permute-start | bytes 24584 | tf_op jit(solution)/shard_map/ppermute | solution.py:18
where the time goes:
time: 393 us; the launch traced here: 392 us
  blocking collectives  154 us (39%)
  waiting for transfers between devices  100 us (25%)
  starting transfers between devices  65.9 us (17%)
  local copies, waits for them, and re-layouts  26.6 us (7%)
  matrix products  26.3 us (7%)
  other arithmetic  18.5 us (5%)
    all_to_all x3, waiting for transfers between devices, exchange(): lax.all_to_all(payload, 'exp', split_axis=0, concat_axis=0, tiled=True)  47.8 us
    all_gather x1, blocking collectives, per_device(): gathered_head = lax.all_gather(scaled_head, 'exp', axis=0, tiled=True)  33.8 us
    all_gather x1, blocking collectives, per_device(): gathered = lax.all_gather(scaled, 'exp', axis=0, tiled=True)  33.7 us
    all_to_all x1, blocking collectives, exchange(): lax.all_to_all(outgoing_rows, 'sky', split_axis=0, concat_axis=0, tiled=T...  31.9 us
    all_gather x1, blocking collectives, per_device(): gathered_tail = lax.all_gather(scaled_tail, 'exp', axis=0, tiled=True)  31.1 us
    all_to_all x1, blocking collectives, fetch(): lax.all_to_all(part.astype(jnp.bfloat16)[safe_rows], 'sky', split_axis=0,...  23.4 us
    all_to_all x1, waiting for transfers between devices, fetch(): lax.all_to_all(part.astype(jnp.bfloat16)[safe_rows], 'sky', split_axis=0,...  23.1 us
    all_to_all x3, starting transfers between devices, exchange(): lax.all_to_all(payload, 'exp', split_axis=0, concat_axis=0, tiled=True)  22.1 us
  transfers between devices with their start and end apart: 12, of which 8 were waited for; matrix products, arithmetic and copies ran while one was open for 6% of the time, Pallas kernels for 0%

commit v1 on v0

--- a/solution.py
+++ b/solution.py
@@ -161,7 +161,14 @@
         scaled_head, outgoing_tail = lax.optimization_barrier(
             (scaled_head, outgoing[:, half_edge:])
         )
-        gathered_head = lax.all_gather(scaled_head, "exp", axis=0, tiled=True)
+        ring = [scaled_head]
+        for hop in range(15):
+            ring.append(lax.ppermute(ring[-1], "exp", [(dev, (dev + 1) % 16) for dev in range(16)]))
+        gathered_head = jnp.roll(
+            jnp.concatenate(ring[::-1], axis=0),
+            (lax.axis_index("exp") + 1) * ring[0].shape[0],
+            axis=0,
+        )
         arrived_tail = lax.all_to_all(outgoing_tail, "sky", split_axis=0, concat_axis=0, tiled=True)
         gathered_head, arrived_tail = lax.optimization_barrier((gathered_head, arrived_tail))
         scaled_tail = gather_scaled(exchange(arrived_tail, None, True), own_denominator)

time: 393 us -> 471 us (1.20)
  waiting for transfers between devices: 100 us -> 178 us
  blocking collectives: 154 us -> 121 us
  starting transfers between devices: 65.9 us -> 96.8 us
    ppermute x0 -> x15, waiting for transfers between devices: none -> 63.7 us  [per_device(): lax.ppermute(ring[-1], 'exp', [(dev, (dev + 1) % 16) for dev in range(16)])]
    all_gather x1 -> x0, blocking collectives: 33.8 us -> none  [per_device(): gathered_head = lax.all_gather(scaled_head, 'exp', axis=0, tiled=True)]
    ppermute x0 -> x15, starting transfers between devices: none -> 29.8 us  [per_device(): lax.ppermute(ring[-1], 'exp', [(dev, (dev + 1) % 16) for dev in range(16)])]
    all_to_all x1, waiting for transfers between devices: 0.01 us -> 15 us  [per_device(): lax.all_to_all(outgoing_tail, 'sky', split_axis=0, concat_axis=0, tiled=T...]
    ppermute x2, waiting for transfers between devices: 6.37 us -> 0.01 us  [padded_2(): lax.ppermute(head, axis, [((i + 1) % count, i) for i in range(ends)])]
  transfers between devices with their start and end apart: 12 -> 27, of which waited for: 8 -> 22; matrix products, arithmetic and copies ran while one was open for 6% -> 5% of each run, Pallas kernels for 0% -> 0%
where the time goes in v1:
time: 471 us; the launch traced here: 469 us
  waiting for transfers between devices  178 us (38%)
  blocking collectives  121 us (26%)
  starting transfers between devices  96.8 us (21%)
  local copies, waits for them, and re-layouts  27.8 us (6%)
  matrix products  26.4 us (6%)
  other arithmetic  18.7 us (4%)
    ppermute x15, waiting for transfers between devices, per_device(): lax.ppermute(ring[-1], 'exp', [(dev, (dev + 1) % 16) for dev in range(16)])  63.7 us
    all_to_all x3, waiting for transfers between devices, exchange(): lax.all_to_all(payload, 'exp', split_axis=0, concat_axis=0, tiled=True)  52.3 us
    all_gather x1, blocking collectives, per_device(): gathered = lax.all_gather(scaled, 'exp', axis=0, tiled=True)  33.6 us
    all_to_all x1, blocking collectives, exchange(): lax.all_to_all(outgoing_rows, 'sky', split_axis=0, concat_axis=0, tiled=T...  31.9 us
    all_gather x1, blocking collectives, per_device(): gathered_tail = lax.all_gather(scaled_tail, 'exp', axis=0, tiled=True)  31.6 us
    ppermute x15, starting transfers between devices, per_device(): lax.ppermute(ring[-1], 'exp', [(dev, (dev + 1) % 16) for dev in range(16)])  29.8 us
    all_to_all x3, starting transfers between devices, exchange(): lax.all_to_all(payload, 'exp', split_axis=0, concat_axis=0, tiled=True)  25.5 us
    all_to_all x1, blocking collectives, fetch(): lax.all_to_all(part.astype(jnp.bfloat16)[safe_rows], 'sky', split_axis=0,...  23.5 us
  transfers between devices with their start and end apart: 27, of which 22 were waited for; matrix products, arithmetic and copies ran while one was open for 5% of the time, Pallas kernels for 0%

profile of v1, /device:TPU:2, one launch (start us, length us, event | category | flops | bytes accessed | tf_op | source)
XLA Modules:
  0.0 469.4 jit_solution(5401360481071644027)
XLA Ops:
  3.8 9.4 %all-to-all-start = ((s32[32,2,1]{1,2,0:T(1,128)}), s32[32,2,1]{1,2,0:T(1,128)S(1)}, u32[]{:S(2)}, u32[]{:S(2)}) async-start(s32[32,2,1]{1,2,0:T(1,128)} %bitcast.2), calls=%async_computation | async-start | bytes 32768 | tf_op jit(solution)/shard_map/all_to_all | solution.py:94
  14.5 4.9 %all-to-all-done = s32[32,2,1]{1,2,0:T(1,128)S(1)} async-done(((s32[32,2,1]{1,2,0:T(1,128)}), s32[32,2,1]{1,2,0:T(1,128)S(1)}, u32[]{:S(2)}, u32[]{:S(2)}) %all-to-all-start) | async-done | bytes 288 | tf_op jit(solution)/shard_map/all_to_all | solution.py:94
  22.9 5.2 %all-to-all-start.1 = ((bf16[64,128,128]{2,1,0:T(8,128)(2,1)}), bf16[64,128,128]{2,1,0:T(8,128)(2,1)S(1)}, u32[]{:S(2)}, u32[]{:S(2)}) async-start(bf16[64,128,128]{2,1,0:T(8,128)(2,1)} %gather_fusion), calls=%async_computation.1 | async-start | bytes 4194304 | tf_op jit(solution)/shard_map/all_to_all | solution.py:123
  33.1 23.1 %all-to-all-done.1 = bf16[64,128,128]{2,1,0:T(8,128)(2,1)S(1)} async-done(((bf16[64,128,128]{2,1,0:T(8,128)(2,1)}), bf16[64,128,128]{2,1,0:T(8,128)(2,1)S(1)}, u32[]{:S(2)}, u32[]{:S(2)}) %all-to-all-start.1) | async-done | bytes 2097184 | tf_op jit(solution)/shard_map/all_to_all | solution.py:123
  56.9 6.4 %fusion.1 = bf16[32,2,128,128]{3,2,1,0:T(8,128)(2,1)} fusion(bf16[1,32,2,128,128]{4,3,2,1,0:T(8,128)(2,1)} %param.8, f32[32,2]{1,0:T(8,128)S(1)} %copy.43, bf16[32,2,2,128,128]{4,3,2,1,0:T(8,128)(2,1)} %bitcast.93, bf16[32,128,128]{2,1,0:T(8,128)(2,1)S(1)} %gather_fusion.1), kind=kOutput, calls=%fused_computation.12 | convolution fusion | flops 542113792 | bytes 9437440 | tf_op jit(solution)/shard_map/fetv,fewv->fetw/dot_general | solution.py:41
  70.1 5.9 %all-to-all-start.2 = ((bf16[64,64,128]{2,1,0:T(8,128)(2,1)}), bf16[64,64,128]{2,1,0:T(8,128)(2,1)S(1)}, u32[]{:S(2)}, u32[]{:S(2)}) async-start(bf16[64,64,128]{2,1,0:T(8,128)(2,1)} %get-tuple-element.30), calls=%async_computation.2 | async-start | bytes 2097152 | tf_op jit(solution)/shard_map/all_to_all | solution.py:110
  76.4 15.9 %all-to-all-done.2 = bf16[64,64,128]{2,1,0:T(8,128)(2,1)S(1)} async-done(((bf16[64,64,128]{2,1,0:T(8,128)(2,1)}), bf16[64,64,128]{2,1,0:T(8,128)(2,1)S(1)}, u32[]{:S(2)}, u32[]{:S(2)}) %all-to-all-start.2) | async-done | bytes 1048608 | tf_op jit(solution)/shard_map/all_to_all | solution.py:110
  93.9 13.3 %all-to-all-start.3 = ((bf16[16,80,128]{2,1,0:T(8,128)(2,1)}), bf16[16,80,128]{2,1,0:T(8,128)(2,1)S(1)}, u32[]{:S(2)}, u32[]{:S(2)}) async-start(bf16[16,80,128]{2,1,0:T(8,128)(2,1)} %copy.47), calls=%async_computation.3 | async-start | bytes 655360 | tf_op jit(solution)/shard_map/all_to_all | solution.py:119
  107.2 21.4 %all-to-all-done.3 = bf16[16,80,128]{2,1,0:T(8,128)(2,1)S(1)} async-done(((bf16[16,80,128]{2,1,0:T(8,128)(2,1)}), bf16[16,80,128]{2,1,0:T(8,128)(2,1)S(1)}, u32[]{:S(2)}, u32[]{:S(2)}) %all-to-all-start.3) | async-done | bytes 327712 | tf_op jit(solution)/shard_map/all_to_all | solution.py:119
  139.6 4.9 %collective-permute-done.1 = bf16[1,64,128]{2,1,0:T(8,128)(2,1)S(1)} collective-permute-done((bf16[1,64,128]{2,1,0:T(8,128)(2,1)S(1)}, bf16[1,64,128]{2,1,0:T(8,128)(2,1)S(1)}, u32[]{:S(2)}, u32[]{:S(2)}) %collective-permute-start.1) | collective-permute-done | bytes 16416 | tf_op jit(solution)/shard_map/ppermute | solution.py:166
  146.5 4.9 %collective-permute-done.2 = bf16[1,64,128]{2,1,0:T(8,128)(2,1)S(1)} collective-permute-done((bf16[1,64,128]{2,1,0:T(8,128)(2,1)S(1)}, bf16[1,64,128]{2,1,0:T(8,128)(2,1)S(1)}, u32[]{:S(2)}, u32[]{:S(2)}) %collective-permute-start.2) | collective-permute-done | bytes 16416 | tf_op jit(solution)/shard_map/ppermute | solution.py:166
  153.3 4.9 %collective-permute-done.3 = bf16[1,64,128]{2,1,0:T(8,128)(2,1)S(1)} collective-permute-done((bf16[1,64,128]{2,1,0:T(8,128)(2,1)S(1)}, bf16[1,64,128]{2,1,0:T(8,128)(2,1)S(1)}, u32[]{:S(2)}, u32[]{:S(2)}) %collective-permute-start.3) | collective-permute-done | bytes 16416 | tf_op jit(solution)/shard_map/ppermute | solution.py:166
  160.1 4.9 %collective-permute-done.4 = bf16[1,64,128]{2,1,0:T(8,128)(2,1)S(1)} collective-permute-done((bf16[1,64,128]{2,1,0:T(8,128)(2,1)S(1)}, bf16[1,64,128]{2,1,0:T(8,128)(2,1)S(1)}, u32[]{:S(2)}, u32[]{:S(2)}) %collective-permute-start.4) | collective-permute-done | bytes 16416 | tf_op jit(solution)/shard_map/ppermute | solution.py:166
  167.0 4.9 %collective-permute-done.5 = bf16[1,64,128]{2,1,0:T(8,128)(2,1)S(1)} collective-permute-done((bf16[1,64,128]{2,1,0:T(8,128)(2,1)S(1)}, bf16[1,64,128]{2,1,0:T(8,128)(2,1)S(1)}, u32[]{:S(2)}, u32[]{:S(2)}) %collective-permute-start.5) | collective-permute-done | bytes 16416 | tf_op jit(solution)/shard_map/ppermute | solution.py:166
  173.8 4.9 %collective-permute-done.6 = bf16[1,64,128]{2,1,0:T(8,128)(2,1)S(1)} collective-permute-done((bf16[1,64,128]{2,1,0:T(8,128)(2,1)S(1)}, bf16[1,64,128]{2,1,0:T(8,128)(2,1)S(1)}, u32[]{:S(2)}, u32[]{:S(2)}) %collective-permute-start.6) | collective-permute-done | bytes 16416 | tf_op jit(solution)/shard_map/ppermute | solution.py:166
  180.6 4.9 %collective-permute-done.7 = bf16[1,64,128]{2,1,0:T(8,128)(2,1)S(1)} collective-permute-done((bf16[1,64,128]{2,1,0:T(8,128)(2,1)S(1)}, bf16[1,64,128]{2,1,0:T(8,128)(2,1)S(1)}, u32[]{:S(2)}, u32[]{:S(2)}) %collective-permute-start.7) | collective-permute-done | bytes 16416 | tf_op jit(solution)/shard_map/ppermute | solution.py:166
  187.5 4.9 %collective-permute-done.8 = bf16[1,64,128]{2,1,0:T(8,128)(2,1)S(1)} collective-permute-done((bf16[1,64,128]{2,1,0:T(8,128)(2,1)S(1)}, bf16[1,64,128]{2,1,0:T(8,128)(2,1)S(1)}, u32[]{:S(2)}, u32[]{:S(2)}) %collective-permute-start.8) | collective-permute-done | bytes 16416 | tf_op jit(solution)/shard_map/ppermute | solution.py:166
  194.3 4.9 %collective-permute-done.9 = bf16[1,64,128]{2,1,0:T(8,128)(2,1)S(1)} collective-permute-done((bf16[1,64,128]{2,1,0:T(8,128)(2,1)S(1)}, bf16[1,64,128]{2,1,0:T(8,128)(2,1)S(1)}, u32[]{:S(2)}, u32[]{:S(2)}) %collective-permute-start.9) | collective-permute-done | bytes 16416 | tf_op jit(solution)/shard_map/ppermute | solution.py:166
  201.1 4.9 %collective-permute-done.10 = bf16[1,64,128]{2,1,0:T(8,128)(2,1)S(1)} collective-permute-done((bf16[1,64,128]{2,1,0:T(8,128)(2,1)S(1)}, bf16[1,64,128]{2,1,0:T(8,128)(2,1)S(1)}, u32[]{:S(2)}, u32[]{:S(2)}) %collective-permute-start.10) | collective-permute-done | bytes 16416 | tf_op jit(solution)/shard_map/ppermute | solution.py:166
  208.0 4.9 %collective-permute-done.11 = bf16[1,64,128]{2,1,0:T(8,128)(2,1)S(1)} collective-permute-done((bf16[1,64,128]{2,1,0:T(8,128)(2,1)S(1)}, bf16[1,64,128]{2,1,0:T(8,128)(2,1)S(1)}, u32[]{:S(2)}, u32[]{:S(2)}) %collective-permute-start.11) | collective-permute-done | bytes 16416 | tf_op jit(solution)/shard_map/ppermute | solution.py:166
  214.8 4.9 %collective-permute-done.12 = bf16[1,64,128]{2,1,0:T(8,128)(2,1)S(1)} collective-permute-done((bf16[1,64,128]{2,1,0:T(8,128)(2,1)S(1)}, bf16[1,64,128]{2,1,0:T(8,128)(2,1)S(1)}, u32[]{:S(2)}, u32[]{:S(2)}) %collective-permute-start.12) | collective-permute-done | bytes 16416 | tf_op jit(solution)/shard_map/ppermute | solution.py:166
  236.8 6.6 %all-to-all-start.4 = ((bf16[64,64,128]{2,1,0:T(8,128)(2,1)}), bf16[64,64,128]{2,1,0:T(8,128)(2,1)}, u32[]{:S(2)}, u32[]{:S(2)}) async-start(bf16[64,64,128]{2,1,0:T(8,128)(2,1)} %get-tuple-element.14), calls=%async_computation.4 | async-start | bytes 2097152 | tf_op jit(solution)/shard_map/all_to_all | solution.py:172
  244.5 15.0 %all-to-all-done.4 = bf16[64,64,128]{2,1,0:T(8,128)(2,1)} async-done(((bf16[64,64,128]{2,1,0:T(8,128)(2,1)}), bf16[64,64,128]{2,1,0:T(8,128)(2,1)}, u32[]{:S(2)}, u32[]{:S(2)}) %all-to-all-start.4) | async-done | bytes 1048608 | tf_op jit(solution)/shard_map/all_to_all | solution.py:172
  262.2 7.8 %all-to-all-start.5 = ((bf16[16,64,128]{2,1,0:T(8,128)(2,1)}), bf16[16,64,128]{2,1,0:T(8,128)(2,1)S(1)}, u32[]{:S(2)}, u32[]{:S(2)}) async-start(bf16[16,64,128]{2,1,0:T(8,128)(2,1)} %copy.53), calls=%async_computation.5 | async-start | bytes 524288 | tf_op jit(solution)/shard_map/all_to_all | solution.py:119
  276.0 12.5 %all-to-all-done.5 = bf16[16,64,128]{2,1,0:T(8,128)(2,1)S(1)} async-done(((bf16[16,64,128]{2,1,0:T(8,128)(2,1)}), bf16[16,64,128]{2,1,0:T(8,128)(2,1)S(1)}, u32[]{:S(2)}, u32[]{:S(2)}) %all-to-all-start.5) | async-done | bytes 262176 | tf_op jit(solution)/shard_map/all_to_all | solution.py:119
  289.3 5.0 %all-to-all-start.6 = ((bf16[64,64,128]{2,1,0:T(8,128)(2,1)}), bf16[64,64,128]{2,1,0:T(8,128)(2,1)S(1)}, u32[]{:S(2)}, u32[]{:S(2)}) async-start(bf16[64,64,128]{2,1,0:T(8,128)(2,1)} %gather_fusion.3), calls=%async_computation.6 | async-start | bytes 2097152 | tf_op jit(solution)/shard_map/all_to_all | solution.py:188
  294.3 31.6 %all_gather.6 = bf16[16,64,128]{2,1,0:T(8,128)(2,1)S(1)} all-gather(bf16[1,64,128]{2,1,0:T(8,128)(2,1)S(1)} %fusion.52), channel_id=1, replica_groups=mesh['exp'=16,'sky'=32] {'exp'}, dimensions={0}, use_global_device_ids=true | all-gather | bytes 278528 | tf_op jit(solution)/shard_map/all_gather | solution.py:187
  329.0 23.5 %all_to_all.51 = bf16[64,64,128]{2,1,0:T(8,128)(2,1)S(1)} all-to-all(bf16[64,64,128]{2,1,0:T(8,128)(2,1)S(1)} %gather_fusion.5), channel_id=1, replica_groups=mesh['exp'=16,'sky'=32] {'sky'}, dimensions={0} | all-to-all | bytes 2097152 | tf_op jit(solution)/shard_map/all_to_all | solution.py:123
  353.2 6.4 %fusion.3 = bf16[32,2,128,128]{3,2,1,0:T(8,128)(2,1)} fusion(bf16[1,32,2,128,128]{4,3,2,1,0:T(8,128)(2,1)} %param.8, f32[32,2]{1,0:T(8,128)S(1)} %copy.43, bf16[32,2,2,128,128]{4,3,2,1,0:T(8,128)(2,1)} %bitcast.95, bf16[32,64,128]{2,1,0:T(8,128)(2,1)S(1)} %gather_fusion.6, bf16[32,64,128]{2,1,0:T(8,128)(2,1)S(1)} %copy-done.4), kind=kOutput, calls=%fused_computation.14 | convolution fusion | flops 544210944 | bytes 9437440 | tf_op jit(solution)/shard_map/fetv,fewv->fetw/dot_general | solution.py:41
  364.9 31.9 %all_to_all.52 = bf16[64,128,128]{2,1,0:T(8,128)(2,1)S(1)} all-to-all(bf16[64,128,128]{2,1,0:T(8,128)(2,1)S(1)} %gather_fusion.7), channel_id=1, replica_groups=mesh['exp'=16,'sky'=32] {'sky'}, dimensions={0} | all-to-all | bytes 4194304 | tf_op jit(solution)/shard_map/all_to_all | solution.py:110
  414.5 18.3 %all-to-all-done.9 = bf16[16,128,128]{2,1,0:T(8,128)(2,1)} async-done(((bf16[16,128,128]{2,1,0:T(8,128)(2,1)}), bf16[16,128,128]{2,1,0:T(8,128)(2,1)}, u32[]{:S(2)}, u32[]{:S(2)}) %all-to-all-start.9) | async-done | bytes 524320 | tf_op jit(solution)/shard_map/all_to_all | solution.py:119
  434.6 33.6 %all-gather = bf16[2048,128]{1,0:T(8,128)(2,1)S(1)} all-gather(bf16[128,128]{1,0:T(8,128)(2,1)S(1)} %divide_convert_fusion), channel_id=2, replica_groups=mesh['exp'=16,'sky'=32] {'exp'}, dimensions={0}, use_global_device_ids=true | all-gather | bytes 557056 | tf_op jit(solution)/shard_map/all_gather | solution.py:156
  (154 shorter events, 112.1 us)
Async XLA Ops:
  3.8 15.6 %all-to-all-start = ((s32[32,2,1]{1,2,0:T(1,128)}), s32[32,2,1]{1,2,0:T(1,128)S(1)}, u32[]{:S(2)}, u32[]{:S(2)}) async-start(s32[32,2,1]{1,2,0:T(1,128)} %bitcast.2), calls=%async_computation | async-start | bytes 32768 | tf_op jit(solution)/shard_map/all_to_all | solution.py:94
  22.9 5.6 %copy-start.5 = (bf16[8,128,128]{2,1,0:T(8,128)(2,1)S(1)}, bf16[8,128,128]{2,1,0:T(8,128)(2,1)}, u32[]{:S(2)}) copy-start(bf16[8,128,128]{2,1,0:T(8,128)(2,1)} %param.13) | copy-start | bytes 786436
  22.9 33.2 %all-to-all-start.1 = ((bf16[64,128,128]{2,1,0:T(8,128)(2,1)}), bf16[64,128,128]{2,1,0:T(8,128)(2,1)S(1)}, u32[]{:S(2)}, u32[]{:S(2)}) async-start(bf16[64,128,128]{2,1,0:T(8,128)(2,1)} %gather_fusion), calls=%async_computation.1 | async-start | bytes 4194304 | tf_op jit(solution)/shard_map/all_to_all | solution.py:123
  70.1 22.2 %all-to-all-start.2 = ((bf16[64,64,128]{2,1,0:T(8,128)(2,1)}), bf16[64,64,128]{2,1,0:T(8,128)(2,1)S(1)}, u32[]{:S(2)}, u32[]{:S(2)}) async-start(bf16[64,64,128]{2,1,0:T(8,128)(2,1)} %get-tuple-element.30), calls=%async_computation.2 | async-start | bytes 2097152 | tf_op jit(solution)/shard_map/all_to_all | solution.py:110
  76.1 145.6 %copy-start = (f32[16,128,128]{2,1,0:T(8,128)S(1)}, f32[16,128,128]{2,1,0:T(8,128)}, u32[]{:S(2)}) copy-start(f32[16,128,128]{2,1,0:T(8,128)} %param.7) | copy-start | bytes 3145732
  93.9 34.7 %all-to-all-start.3 = ((bf16[16,80,128]{2,1,0:T(8,128)(2,1)}), bf16[16,80,128]{2,1,0:T(8,128)(2,1)S(1)}, u32[]{:S(2)}, u32[]{:S(2)}) async-start(bf16[16,80,128]{2,1,0:T(8,128)(2,1)} %copy.47), calls=%async_computation.3 | async-start | bytes 655360 | tf_op jit(solution)/shard_map/all_to_all | solution.py:119
  130.1 7.6 %collective-permute-start = (bf16[1,64,128]{2,1,0:T(8,128)(2,1)S(1)}, bf16[1,64,128]{2,1,0:T(8,128)(2,1)S(1)}, u32[]{:S(2)}, u32[]{:S(2)}) collective-permute-start(bf16[1,64,128]{2,1,0:T(8,128)(2,1)S(1)} %fusion.53), channel_id=1, source_target_pairs={{0,32},{32,64},{64,96},{96,128},{128,160},{160,192},{192,224},{224... | collective-permute-start | bytes 49160 | tf_op jit(solution)/shard_map/ppermute | solution.py:166
  137.7 6.8 %collective-permute-start.1 = (bf16[1,64,128]{2,1,0:T(8,128)(2,1)S(1)}, bf16[1,64,128]{2,1,0:T(8,128)(2,1)S(1)}, u32[]{:S(2)}, u32[]{:S(2)}) collective-permute-start(bf16[1,64,128]{2,1,0:T(8,128)(2,1)S(1)} %collective-permute-done), channel_id=1, source_target_pairs={{0,32},{32,64},{64,96},{96,128},{128,160},{160,192},{192,224},{224... | collective-permute-start | bytes 49160 | tf_op jit(solution)/shard_map/ppermute | solution.py:166
  144.6 6.8 %collective-permute-start.2 = (bf16[1,64,128]{2,1,0:T(8,128)(2,1)S(1)}, bf16[1,64,128]{2,1,0:T(8,128)(2,1)S(1)}, u32[]{:S(2)}, u32[]{:S(2)}) collective-permute-start(bf16[1,64,128]{2,1,0:T(8,128)(2,1)S(1)} %collective-permute-done.1), channel_id=1, source_target_pairs={{0,32},{32,64},{64,96},{96,128},{128,160},{160,192},{192,224},{224... | collective-permute-start | bytes 49160 | tf_op jit(solution)/shard_map/ppermute | solution.py:166
  151.4 6.8 %collective-permute-start.3 = (bf16[1,64,128]{2,1,0:T(8,128)(2,1)S(1)}, bf16[1,64,128]{2,1,0:T(8,128)(2,1)S(1)}, u32[]{:S(2)}, u32[]{:S(2)}) collective-permute-start(bf16[1,64,128]{2,1,0:T(8,128)(2,1)S(1)} %collective-permute-done.2), channel_id=1, source_target_pairs={{0,32},{32,64},{64,96},{96,128},{128,160},{160,192},{192,224},{224... | collective-permute-start | bytes 49160 | tf_op jit(solution)/shard_map/ppermute | solution.py:166
  158.2 6.8 %collective-permute-start.4 = (bf16[1,64,128]{2,1,0:T(8,128)(2,1)S(1)}, bf16[1,64,128]{2,1,0:T(8,128)(2,1)S(1)}, u32[]{:S(2)}, u32[]{:S(2)}) collective-permute-start(bf16[1,64,128]{2,1,0:T(8,128)(2,1)S(1)} %collective-permute-done.3), channel_id=1, source_target_pairs={{0,32},{32,64},{64,96},{96,128},{128,160},{160,192},{192,224},{224... | collective-permute-start | bytes 49160 | tf_op jit(solution)/shard_map/ppermute | solution.py:166
  165.1 6.8 %collective-permute-start.5 = (bf16[1,64,128]{2,1,0:T(8,128)(2,1)S(1)}, bf16[1,64,128]{2,1,0:T(8,128)(2,1)S(1)}, u32[]{:S(2)}, u32[]{:S(2)}) collective-permute-start(bf16[1,64,128]{2,1,0:T(8,128)(2,1)S(1)} %collective-permute-done.4), channel_id=1, source_target_pairs={{0,32},{32,64},{64,96},{96,128},{128,160},{160,192},{192,224},{224... | collective-permute-start | bytes 49160 | tf_op jit(solution)/shard_map/ppermute | solution.py:166
  171.9 6.8 %collective-permute-start.6 = (bf16[1,64,128]{2,1,0:T(8,128)(2,1)S(1)}, bf16[1,64,128]{2,1,0:T(8,128)(2,1)S(1)}, u32[]{:S(2)}, u32[]{:S(2)}) collective-permute-start(bf16[1,64,128]{2,1,0:T(8,128)(2,1)S(1)} %collective-permute-done.5), channel_id=1, source_target_pairs={{0,32},{32,64},{64,96},{96,128},{128,160},{160,192},{192,224},{224... | collective-permute-start | bytes 49160 | tf_op jit(solution)/shard_map/ppermute | solution.py:166
  178.7 6.8 %collective-permute-start.7 = (bf16[1,64,128]{2,1,0:T(8,128)(2,1)S(1)}, bf16[1,64,128]{2,1,0:T(8,128)(2,1)S(1)}, u32[]{:S(2)}, u32[]{:S(2)}) collective-permute-start(bf16[1,64,128]{2,1,0:T(8,128)(2,1)S(1)} %collective-permute-done.6), channel_id=1, source_target_pairs={{0,32},{32,64},{64,96},{96,128},{128,160},{160,192},{192,224},{224... | collective-permute-start | bytes 49160 | tf_op jit(solution)/shard_map/ppermute | solution.py:166
  185.6 6.8 %collective-permute-start.8 = (bf16[1,64,128]{2,1,0:T(8,128)(2,1)S(1)}, bf16[1,64,128]{2,1,0:T(8,128)(2,1)S(1)}, u32[]{:S(2)}, u32[]{:S(2)}) collective-permute-start(bf16[1,64,128]{2,1,0:T(8,128)(2,1)S(1)} %collective-permute-done.7), channel_id=1, source_target_pairs={{0,32},{32,64},{64,96},{96,128},{128,160},{160,192},{192,224},{224... | collective-permute-start | bytes 49160 | tf_op jit(solution)/shard_map/ppermute | solution.py:166
  192.4 6.8 %collective-permute-start.9 = (bf16[1,64,128]{2,1,0:T(8,128)(2,1)S(1)}, bf16[1,64,128]{2,1,0:T(8,128)(2,1)S(1)}, u32[]{:S(2)}, u32[]{:S(2)}) collective-permute-start(bf16[1,64,128]{2,1,0:T(8,128)(2,1)S(1)} %collective-permute-done.8), channel_id=1, source_target_pairs={{0,32},{32,64},{64,96},{96,128},{128,160},{160,192},{192,224},{224... | collective-permute-start | bytes 49160 | tf_op jit(solution)/shard_map/ppermute | solution.py:166
  199.2 6.8 %collective-permute-start.10 = (bf16[1,64,128]{2,1,0:T(8,128)(2,1)S(1)}, bf16[1,64,128]{2,1,0:T(8,128)(2,1)S(1)}, u32[]{:S(2)}, u32[]{:S(2)}) collective-permute-start(bf16[1,64,128]{2,1,0:T(8,128)(2,1)S(1)} %collective-permute-done.9), channel_id=1, source_target_pairs={{0,32},{32,64},{64,96},{96,128},{128,160},{160,192},{192,224},{224... | collective-permute-start | bytes 49160 | tf_op jit(solution)/shard_map/ppermute | solution.py:166
  206.1 6.8 %collective-permute-start.11 = (bf16[1,64,128]{2,1,0:T(8,128)(2,1)S(1)}, bf16[1,64,128]{2,1,0:T(8,128)(2,1)S(1)}, u32[]{:S(2)}, u32[]{:S(2)}) collective-permute-start(bf16[1,64,128]{2,1,0:T(8,128)(2,1)S(1)} %collective-permute-done.10), channel_id=1, source_target_pairs={{0,32},{32,64},{64,96},{96,128},{128,160},{160,192},{192,224},{224... | collective-permute-start | bytes 49160 | tf_op jit(solution)/shard_map/ppermute | solution.py:166
  212.9 6.8 %collective-permute-start.12 = (bf16[1,64,128]{2,1,0:T(8,128)(2,1)S(1)}, bf16[1,64,128]{2,1,0:T(8,128)(2,1)S(1)}, u32[]{:S(2)}, u32[]{:S(2)}) collective-permute-start(bf16[1,64,128]{2,1,0:T(8,128)(2,1)S(1)} %collective-permute-done.11), channel_id=1, source_target_pairs={{0,32},{32,64},{64,96},{96,128},{128,160},{160,192},{192,224},{224... | collective-permute-start | bytes 49160 | tf_op jit(solution)/shard_map/ppermute | solution.py:166
  219.7 11.2 %collective-permute-start.13 = (bf16[1,64,128]{2,1,0:T(8,128)(2,1)S(1)}, bf16[1,64,128]{2,1,0:T(8,128)(2,1)S(1)}, u32[]{:S(2)}, u32[]{:S(2)}) collective-permute-start(bf16[1,64,128]{2,1,0:T(8,128)(2,1)S(1)} %collective-permute-done.12), channel_id=1, source_target_pairs={{0,32},{32,64},{64,96},{96,128},{128,160},{160,192},{192,224},{224... | collective-permute-start | bytes 49160 | tf_op jit(solution)/shard_map/ppermute | solution.py:166
  222.3 4.7 %collective-permute-start.16 = (f32[16,128,1]{1,0,2:T(8,128)S(1)}, f32[16,128,1]{1,0,2:T(8,128)S(1)}, u32[]{:S(2)}, u32[]{:S(2)}) collective-permute-start(f32[16,128,1]{1,0,2:T(8,128)S(1)} %copy.70), channel_id=1, source_target_pairs={{1,0},{2,1},{3,2},{4,3},{5,4},{6,5},{7,6},{8,7},{9,8},{10,9},{11,1... | collective-permute-start | bytes 24584 | tf_op jit(solution)/shard_map/ppermute | solution.py:20
  224.6 5.0 %collective-permute-start.15 = (f32[16,128,1]{1,0,2:T(8,128)S(1)}, f32[16,128,1]{1,0,2:T(8,128)S(1)}, u32[]{:S(2)}, u32[]{:S(2)}) collective-permute-start(f32[16,128,1]{1,0,2:T(8,128)S(1)} %copy.69), channel_id=1, source_target_pairs={{0,1},{1,2},{2,3},{3,4},{4,5},{5,6},{6,7},{7,8},{8,9},{9,10},{10,1... | collective-permute-start | bytes 24584 | tf_op jit(solution)/shard_map/ppermute | solution.py:18
  230.9 12.4 %collective-permute-start.14 = (bf16[1,64,128]{2,1,0:T(8,128)(2,1)S(1)}, bf16[1,64,128]{2,1,0:T(8,128)(2,1)S(1)}, u32[]{:S(2)}, u32[]{:S(2)}) collective-permute-start(bf16[1,64,128]{2,1,0:T(8,128)(2,1)S(1)} %collective-permute-done.13), channel_id=1, source_target_pairs={{0,32},{32,64},{64,96},{96,128},{128,160},{160,192},{192,224},{224... | collective-permute-start | bytes 49160 | tf_op jit(solution)/shard_map/ppermute | solution.py:166
  236.8 22.8 %all-to-all-start.4 = ((bf16[64,64,128]{2,1,0:T(8,128)(2,1)}), bf16[64,64,128]{2,1,0:T(8,128)(2,1)}, u32[]{:S(2)}, u32[]{:S(2)}) async-start(bf16[64,64,128]{2,1,0:T(8,128)(2,1)} %get-tuple-element.14), calls=%async_computation.4 | async-start | bytes 2097152 | tf_op jit(solution)/shard_map/all_to_all | solution.py:172
  262.2 26.3 %all-to-all-start.5 = ((bf16[16,64,128]{2,1,0:T(8,128)(2,1)}), bf16[16,64,128]{2,1,0:T(8,128)(2,1)S(1)}, u32[]{:S(2)}, u32[]{:S(2)}) async-start(bf16[16,64,128]{2,1,0:T(8,128)(2,1)} %copy.53), calls=%async_computation.5 | async-start | bytes 524288 | tf_op jit(solution)/shard_map/all_to_all | solution.py:119
  289.3 36.6 %all-to-all-start.6 = ((bf16[64,64,128]{2,1,0:T(8,128)(2,1)}), bf16[64,64,128]{2,1,0:T(8,128)(2,1)S(1)}, u32[]{:S(2)}, u32[]{:S(2)}) async-start(bf16[64,64,128]{2,1,0:T(8,128)(2,1)} %gather_fusion.3), calls=%async_computation.6 | async-start | bytes 2097152 | tf_op jit(solution)/shard_map/all_to_all | solution.py:188
  329.0 24.2 %copy-start.4 = (bf16[32,64,128]{2,1,0:T(8,128)(2,1)S(1)}, bf16[32,64,128]{2,1,0:T(8,128)(2,1)}, u32[]{:S(2)}) copy-start(bf16[32,64,128]{2,1,0:T(8,128)(2,1)} %gather_fusion.4) | copy-start | bytes 1572868
  396.8 6.6 %copy-start.1 = (f32[16,64,128]{2,1,0:T(8,128)S(1)}, f32[16,64,128]{2,1,0:T(8,128)}, u32[]{:S(2)}) copy-start(f32[16,64,128]{2,1,0:T(8,128)} %get-tuple-element.28) | copy-start | bytes 1572868
  396.8 6.6 %copy-start.2 = (f32[16,64,128]{2,1,0:T(8,128)S(1)}, f32[16,64,128]{2,1,0:T(8,128)}, u32[]{:S(2)}) copy-start(f32[16,64,128]{2,1,0:T(8,128)} %get-tuple-element.26) | copy-start | bytes 1572868
  399.0 33.8 %all-to-all-start.9 = ((bf16[16,128,128]{2,1,0:T(8,128)(2,1)}), bf16[16,128,128]{2,1,0:T(8,128)(2,1)}, u32[]{:S(2)}, u32[]{:S(2)}) async-start(bf16[16,128,128]{2,1,0:T(8,128)(2,1)} %copy.56), calls=%async_computation.9 | async-start | bytes 1048576 | tf_op jit(solution)/shard_map/all_to_all | solution.py:119
  404.1 5.4 %collective-permute-start.18 = (f32[16,128,1]{1,0,2:T(8,128)S(1)}, f32[16,128,1]{1,0,2:T(8,128)S(1)}, u32[]{:S(2)}, u32[]{:S(2)}) collective-permute-start(f32[16,128,1]{1,0,2:T(8,128)S(1)} %copy.58), channel_id=1, source_target_pairs={{1,0},{2,1},{3,2},{4,3},{5,4},{6,5},{7,6},{8,7},{9,8},{10,9},{11,1... | collective-permute-start | bytes 24584 | tf_op jit(solution)/shard_map/ppermute | solution.py:20
  407.4 5.0 %collective-permute-start.17 = (f32[16,128,1]{1,0,2:T(8,128)S(1)}, f32[16,128,1]{1,0,2:T(8,128)S(1)}, u32[]{:S(2)}, u32[]{:S(2)}) collective-permute-start(f32[16,128,1]{1,0,2:T(8,128)S(1)} %copy.57), channel_id=1, source_target_pairs={{0,1},{1,2},{2,3},{3,4},{4,5},{5,6},{6,7},{7,8},{8,9},{9,10},{10,1... | collective-permute-start | bytes 24584 | tf_op jit(solution)/shard_map/ppermute | solution.py:18
  (4 other events, 14.8 us)
